TPU v7x, 32 devices: a whole 2x2x4 slice. The times are simulated.
32 devices in a mesh: store: 4 (over x, core), blk: 2 (over y), batch: 4 (over z).
Axes of the slice: x: 2, y: 2, z: 4, core: 2. Of those that a mesh axis runs over, the one named last changes fastest.
Arguments:
- cands: bfloat16 [16, 256, 1024], P(('batch', 'store'), 'blk'), parts along dimension 0, may hold values from -6 to 6
- kv_store: bfloat16 [16, 512, 2, 1024], P('batch', ('blk', 'store')), parts along dimension 0, may hold values from -6 to 6
- proj_weight: bfloat16 [1024, 2, 1024], P(None, None, 'blk'), may hold values from -0.1875 to 0.1875
- norm_gain: float32 [1024], replicated, may hold values from 0.5 to 1.5
- users: int32 [16], P('batch'), parts along dimension 0, may hold values from 0 to 3, each once
- lengths: int32 [16], P('batch'), parts along dimension 0, may hold values from 128 to 512, as said below
Outputs:
- scored: bfloat16 [16, 256, 1024], P(('batch', 'store'), 'blk'), parts along dimension 0
There are 4 independent parts, one for each index of `batch`. A program takes and returns all parts, laid end to end along the dimension named above; an argument that names none is the same for every part. Nothing has to cross between parts.
Inputs may be any that keep to these rules, and one draw needn't show every extreme that they name: A permutation of the users. `lengths`: some user has all 512 events live.
All inputs are finite; a program needn't handle non-finite values.
Results may differ from a plain program's by a relative error of at most 0.014.
Values may be sent and summed in bfloat16 or wider, within the bound.
No kernel may reach another device: no remote copies, remote signals or barrier semaphores. Data moves between devices by JAX's collectives and lax.ppermute only.
A program may use at most 64 MiB of HBM per device.

v0:
```python
import jax
import jax.numpy as jnp
from jax import lax
from jax.sharding import PartitionSpec as P

D = 1024
HEADS = 8


def attend(query, keys, values, offset, count):
    head_size = D // HEADS
    inverse = head_size ** (-0.5)
    rows = query.shape[0]
    local_heads = query.shape[1] // head_size
    total = keys.shape[0]
    block = min(total, 256)
    qheads = query.reshape(rows, local_heads, head_size)
    scale_count = count.astype(jnp.float32)

    def one_block(index, accum):
        start = index * block
        key_block = lax.dynamic_slice_in_dim(keys, start, block, 0).reshape(
            block, local_heads, head_size
        )
        value_block = lax.dynamic_slice_in_dim(values, start, block, 0).reshape(
            block, local_heads, head_size
        )
        scores = (
            jnp.einsum("chd,khd->hck", qheads, key_block, preferred_element_type=jnp.float32)
            * inverse
        )
        live = (offset + start + jnp.arange(block) < count).astype(jnp.float32)
        weights = (jax.nn.silu(scores) * live[None, None, :] / scale_count).astype(jnp.bfloat16)
        part_sum = jnp.einsum(
            "hck,khd->chd", weights, value_block, preferred_element_type=jnp.float32
        )
        return accum + part_sum.reshape(rows, local_heads * head_size)

    empty = jnp.zeros((rows, local_heads * head_size), jnp.float32)
    return lax.fori_loop(0, total // block, one_block, empty)


def finish(attended, gate, norm_gain):
    wide = attended.astype(jnp.float32)
    mean = jnp.mean(wide, axis=1, keepdims=True)
    var = jnp.mean((wide - mean) ** 2, axis=1, keepdims=True)
    normed = (wide - mean) * lax.rsqrt(var + 1e-05) * norm_gain[None, :]
    return (normed * gate.astype(jnp.float32)).astype(jnp.bfloat16)


def per_device(cands, kv_store, proj_weight, norm_gain, users, lengths):
    slot = lax.axis_index("store")
    person = lax.dynamic_index_in_dim(users, slot, 0, keepdims=False)
    count = lax.dynamic_index_in_dim(lengths, person, 0, keepdims=False)
    ordered = jnp.take(kv_store, users, axis=0)
    feats = cands[0]
    fetched = lax.all_to_all(ordered, "store", split_axis=0, concat_axis=1, tiled=True)
    keys = fetched[0, :, 0, :]
    values = fetched[0, :, 1, :]
    offset = lax.axis_index("blk") * keys.shape[0]
    full_weight = lax.all_gather(proj_weight, "blk", axis=2, tiled=True)
    width = full_weight.shape[0]
    own_proj = jnp.dot(
        feats, full_weight.reshape(width, 2 * width), preferred_element_type=jnp.float32
    )
    own_query = own_proj[:, :width].astype(jnp.bfloat16)
    gate = jax.nn.silu(own_proj[:, width:]).astype(jnp.bfloat16)
    query = lax.all_gather(own_query, "blk", axis=0, tiled=True)
    attended = lax.psum_scatter(
        attend(query, keys, values, offset, count), "blk", scatter_dimension=0, tiled=True
    ).astype(jnp.bfloat16)
    return finish(attended, gate, norm_gain)[None]


def solution(mesh):
    in_specs = (
        P(("batch", "store"), "blk", None),
        P("batch", ("blk", "store"), None, None),
        P(None, None, "blk"),
        P(),
        P("batch"),
        P("batch"),
    )
    out_specs = P(("batch", "store"), "blk", None)
    return jax.shard_map(
        per_device, mesh=mesh, in_specs=in_specs, out_specs=out_specs, check_vma=False
    )
```

profile of v0, /device:TPU:0, one launch (start us, length us, event | category | flops | bytes accessed | tf_op | source)
XLA Modules:
  0.0 117.1 jit_solution(7535598614453149541)
XLA Ops:
  6.5 0.7 all-gather.2.cloned.1.call-update
  7.3 0.0 copy-done.3
  7.3 0.5 copy-done
  7.8 2.7 %gather_fusion = bf16[4,64,2,1024]{3,2,1,0:T(2,128)(2,1)S(1)} fusion(bf16[4,64,2,1024]{3,2,1,0:T(2,128)(2,1)S(1)} %copy-done, s32[1024]{0:T(1024)S(1)} %pad_clamp_fusion), kind=kCustom, calls=%fused_computation | custom fusion | bytes 2097168 | tf_op jit(solution)/shard_map/jit(_take)/gather | solution.py:55
  10.5 1.9 %broadcast_select_fusion = bf16[4,64,2,1024]{3,2,1,0:T(2,128)(2,1)} fusion(bf16[4,64,2,1024]{3,2,1,0:T(2,128)(2,1)S(1)} %gather_fusion, pred[4]{0:T(512)(128)(4,1)S(1)} %compare_and_fusion), kind=kLoop, calls=%fused_computation.2 | loop fusion | flops 524288 | bytes 2097156 | tf_op jit(solution)/shard_map/jit(_take)/select_n | solution.py:55
  12.4 4.2 %all-to-all-start = ((bf16[4,64,2,1024]{3,2,1,0:T(2,128)(2,1)}), bf16[4,64,2,1024]{3,2,1,0:T(2,128)(2,1)S(1)}, u32[]{:S(2)}, u32[]{:S(2)}) async-start(bf16[4,64,2,1024]{3,2,1,0:T(2,128)(2,1)} %broadcast_select_fusion), calls=%async_computation | async-start | bytes 2097152 | tf_op jit(solution)/shard_map/all_to_all | solution.py:57
  16.6 0.6 dynamic_slice.11
  19.2 0.6 dynamic_slice.12
  20.4 0.7 compare_convert_fusion
  21.1 10.0 %all-to-all-done = bf16[4,64,2,1024]{3,2,1,0:T(2,128)(2,1)S(1)} async-done(((bf16[4,64,2,1024]{3,2,1,0:T(2,128)(2,1)}), bf16[4,64,2,1024]{3,2,1,0:T(2,128)(2,1)S(1)}, u32[]{:S(2)}, u32[]{:S(2)}) %all-to-all-start) | async-done | bytes 1048608 | tf_op jit(solution)/shard_map/all_to_all | solution.py:57
  31.1 0.3 copy.19
  31.4 0.1 fusion.20
  31.4 1.0 copy.20
  32.5 1.0 copy.21
  33.5 34.9 %all-gather.2.cloned.1.call-done = bf16[1024,2,1024]{2,1,0:T(2,128)(2,1)} async-done(((bf16[1024,2,512]{2,1,0:T(2,128)(2,1)}), bf16[1024,2,1024]{2,1,0:T(2,128)(2,1)}) %all-gather.2.cloned.1.call-update) | async-done | bytes 4194320 | tf_op jit(solution)/shard_map/all_gather | solution.py:61
  68.3 3.7 %copy.28 = bf16[128,8,2,1024]{3,1,2,0:T(8,128)(2,1)S(1)} copy(bf16[128,8,2,1024]{3,2,1,0:T(2,128)(2,1)} %bitcast.28) | data formatting | bytes 8388608
  72.0 0.7 fusion.15
  72.8 8.8 %all_gather.7 = bf16[256,1024]{1,0:T(8,128)(2,1)} all-gather(bf16[128,1024]{1,0:T(8,128)(2,1)S(1)} %slice.29), channel_id=1, replica_groups=mesh['store'=4,'blk'=2,'batch'=4] {'blk'}, dimensions={0}, use_global_device_ids=true | all-gather | bytes 786432 | tf_op jit(solution)/shard_map/all_gather | solution.py:68
  81.6 2.4 %fusion = f32[8,128,256]{2,1,0:T(8,128)S(1)} fusion(bf16[256,8,128]{0,2,1:T(8,128)(2,1)} %bitcast.31, bf16[256,8,128]{0,2,1:T(8,128)(2,1)} %bitcast.32, f32[]{:T(128)S(6)} %convert_element_type.32, f32[256]{0:T(256)S(1)} %compare_convert_fusion, bf16[256,1024]{1,0:T(8,128)(2,1)} %all_gather.7), kind=kOutput, calls=%fused_computation.3 | convolution fusion | flops 272629760 | bytes 2622468 | tf_op jit(solution)/shard_map/while/body/eval_jaxpr/hck,khd->chd/dot_general | solution.py:34
  84.1 1.3 %copy.26 = f32[256,1024]{1,0:T(8,128)} copy(f32[256,1024]{0,1:T(8,128)S(1)} %bitcast.30) | data formatting | bytes 2097152 | tf_op jit(solution)/shard_map/while/body/eval_jaxpr/reshape | solution.py:37
  85.4 20.5 %reduce-scatter.2.cloned.1.call-done = f32[128,1024]{1,0:T(8,128)} async-done(((f32[256,1024]{1,0:T(8,128)}), f32[128,1024]{1,0:T(8,128)}) %reduce-scatter.2.cloned.1.call-update) | async-done | bytes 524304 | tf_op jit(solution)/shard_map/reduce_scatter | solution.py:69
  105.9 1.1 convert_reduce_fusion
  107.1 1.2 %fusion.7 = f32[128]{0:T(128)S(1)} fusion(f32[128]{0:T(128)S(1)} %broadcast_multiply_fusion, f32[128,1024]{1,0:T(8,128)} %reduce-scatter.2.cloned.1.call-done), kind=kLoop, calls=%fused_computation.12 | loop fusion | flops 655232 | bytes 525312 | tf_op jit(solution)/shard_map/reduce_sum | solution.py:46
  108.3 2.0 %fusion.17 = bf16[1,128,1024]{2,1,0:T(8,128)(2,1)} fusion(f32[128,2048]{1,0:T(8,128)S(1)} %fusion.15, f32[1024]{0:T(1024)S(1)} %copy-done.2, f32[128]{0:T(128)S(1)} %add_rsqrt_fusion, f32[128]{0:T(128)S(1)} %broadcast_multiply_fusion, f32[128,1024]{1,0:T(8,128)} %reduce-scatter.2.cloned.1.call-done), kind=kLoop, calls=%fused_computation.22 | loop fusion | flops 1703936 | bytes 1315840 | tf_op jit(solution)/shard_map/broadcast_in_dim | solution.py:72
  (17 shorter events, 0.1 us)
Async XLA Ops:
  6.5 1.2 %copy-start = (bf16[4,64,2,1024]{3,2,1,0:T(2,128)(2,1)S(1)}, bf16[4,64,2,1024]{3,2,1,0:T(2,128)(2,1)}, u32[]{:S(2)}) copy-start(bf16[4,64,2,1024]{3,2,1,0:T(2,128)(2,1)} %param.7) | copy-start | bytes 3145732
  6.5 0.7 copy-start.3
  6.5 61.8 %all-gather.2.cloned.1.call-start = ((), (), s32[]{:S(2)}) async-start(), calls=%async_computation.2 | async-start | bytes 6291456 | tf_op jit(solution)/shard_map/all_gather | solution.py:61
  10.5 8.7 %copy-start.4 = (s32[4]{0:T(128)S(1)}, s32[4]{0:T(128)}, u32[]{:S(2)}) copy-start(s32[4]{0:T(128)} %param.11) | copy-start | bytes 52
  12.4 18.7 %all-to-all-start = ((bf16[4,64,2,1024]{3,2,1,0:T(2,128)(2,1)}), bf16[4,64,2,1024]{3,2,1,0:T(2,128)(2,1)S(1)}, u32[]{:S(2)}, u32[]{:S(2)}) async-start(bf16[4,64,2,1024]{3,2,1,0:T(2,128)(2,1)} %broadcast_select_fusion), calls=%async_computation | async-start | bytes 2097152 | tf_op jit(solution)/shard_map/all_to_all | solution.py:57
  16.6 89.3 %reduce-scatter.2.cloned.1.call-start = ((), (), s32[]{:S(2)}) async-start(), calls=%async_computation.3 | async-start | bytes 1572864 | tf_op jit(solution)/shard_map/reduce_scatter | solution.py:69
  68.3 3.7 %copy-start.1 = (bf16[1,128,1024]{2,1,0:T(8,128)(2,1)S(1)}, bf16[1,128,1024]{2,1,0:T(8,128)(2,1)}, u32[]{:S(2)}) copy-start(bf16[1,128,1024]{2,1,0:T(8,128)(2,1)} %param.6) | copy-start | bytes 786436
  84.1 24.2 %copy-start.2 = (f32[1024]{0:T(1024)S(1)}, f32[1024]{0:T(1024)}, u32[]{:S(2)}) copy-start(f32[1024]{0:T(1024)} %param.9) | copy-start | bytes 12292
Sparse Core Ops, SparseCore 0:
  8.9 59.4 all-gather.1
  85.5 20.3 reduce-scatter.1
where the time goes:
time: 118 us; the launch traced here: 117 us
  waiting for transfers between devices  66.1 us (56%)
  between operations  16.1 us (14%)
  local copies, waits for them, and re-layouts  11.7 us (10%)
  blocking collectives  8.83 us (7%)
  other arithmetic  7 us (6%)
  starting transfers between devices  4.21 us (4%)
  matrix products  3.16 us (3%)
    all_gather x1, waiting for transfers between devices, per_device(): full_weight = lax.all_gather(proj_weight, 'blk', axis=2, tiled=True)  34.9 us
    reduce_scatter x1, waiting for transfers between devices, per_device(): lax.psum_scatter(attend(query, keys, values, offset, count), 'blk', scatt...  20.5 us
    all_to_all x1, waiting for transfers between devices, per_device(): lax.all_to_all(ordered, 'store', split_axis=0, concat_axis=1, tiled=True)  9.99 us
    all_gather x1, blocking collectives, per_device(): query = lax.all_gather(own_query, 'blk', axis=0, tiled=True)  8.83 us
    all_to_all x1, starting transfers between devices, per_device(): lax.all_to_all(ordered, 'store', split_axis=0, concat_axis=1, tiled=True)  4.21 us
    unnamed x11, local copies, waits for them, and re-layouts  4.18 us
    gather x1, local copies, waits for them, and re-layouts, per_device(): ordered = jnp.take(kv_store, users, axis=0)  2.65 us
    dot_general x1, matrix products, one_block(): jnp.einsum('hck,khd->chd', weights, value_block, preferred_element_type=j...  2.44 us
  transfers between devices with their start and end apart: 3, of which 3 were waited for; matrix products, arithmetic and copies ran while one was open for 8% of the time, Pallas kernels for 0%

commit v1 on v0

--- a/solution.py
+++ b/solution.py
@@ -5,6 +5,18 @@
 
 D = 1024
 HEADS = 8
+
+
+def collect(value, axis, dim):
+    ways, here = (lax.axis_size(axis), lax.axis_index(axis))
+    grown, reach = (value, 1)
+    while reach < ways:
+        theirs = lax.ppermute(grown, axis, [(d, d ^ reach) for d in range(ways)])
+        mine_first = jnp.concatenate([grown, theirs], axis=dim)
+        theirs_first = jnp.concatenate([theirs, grown], axis=dim)
+        grown = jnp.where(here & reach == 0, mine_first, theirs_first)
+        reach = 2 * reach
+    return grown
 
 
 def attend(query, keys, values, offset, count):
@@ -58,7 +70,7 @@
     keys = fetched[0, :, 0, :]
     values = fetched[0, :, 1, :]
     offset = lax.axis_index("blk") * keys.shape[0]
-    full_weight = lax.all_gather(proj_weight, "blk", axis=2, tiled=True)
+    full_weight = collect(proj_weight, "blk", 2)
     width = full_weight.shape[0]
     own_proj = jnp.dot(
         feats, full_weight.reshape(width, 2 * width), preferred_element_type=jnp.float32

time: 118 us -> 111 us (0.941)
  waiting for transfers between devices: 66.1 us -> 52 us
  other arithmetic: 7 us -> 15.8 us
  local copies, waits for them, and re-layouts: 11.7 us -> 7.71 us
  starting transfers between devices: 4.21 us -> 6.52 us
  matrix products: 3.16 us -> 4.5 us
    all_gather x1 -> x0, waiting for transfers between devices: 34.9 us -> none  [per_device(): full_weight = lax.all_gather(proj_weight, 'blk', axis=2, tiled=True)]
    ppermute x0 -> x1, waiting for transfers between devices: none -> 20.5 us  [collect(): theirs = lax.ppermute(grown, axis, [(d, d ^ reach) for d in range(ways)])]
    select_n x0 -> x1, other arithmetic: none -> 8.19 us  [collect(): grown = jnp.where(here & reach == 0, mine_first, theirs_first)]
    ppermute x0 -> x1, starting transfers between devices: none -> 2.97 us  [collect(): theirs = lax.ppermute(grown, axis, [(d, d ^ reach) for d in range(ways)])]
    unnamed x11, local copies, waits for them, and re-layouts: 4.18 us -> 1.45 us
    reshape x1 -> x0, local copies, waits for them, and re-layouts: 1.31 us -> none  [one_block(): return accum + part_sum.reshape(rows, local_heads * head_size)]
where the time goes in v1:
time: 111 us
  waiting for transfers between devices  52 us (47%)
  between operations  16.1 us (15%)
  other arithmetic  15.8 us (14%)
  blocking collectives  8.2 us (7%)
  local copies, waits for them, and re-layouts  7.71 us (7%)
  starting transfers between devices  6.52 us (6%)
  matrix products  4.5 us (4%)
    reduce_scatter x1, waiting for transfers between devices, per_device(): lax.psum_scatter(attend(query, keys, values, offset, count), 'blk', scatt...  21.6 us
    ppermute x1, waiting for transfers between devices, collect(): theirs = lax.ppermute(grown, axis, [(d, d ^ reach) for d in range(ways)])  20.5 us
    all_to_all x1, waiting for transfers between devices, per_device(): lax.all_to_all(ordered, 'store', split_axis=0, concat_axis=1, tiled=True)  9.92 us
    all_gather x1, blocking collectives, per_device(): query = lax.all_gather(own_query, 'blk', axis=0, tiled=True)  8.2 us
    select_n x1, other arithmetic, collect(): grown = jnp.where(here & reach == 0, mine_first, theirs_first)  8.19 us
    all_to_all x1, starting transfers between devices, per_device(): lax.all_to_all(ordered, 'store', split_axis=0, concat_axis=1, tiled=True)  3.51 us
    dot_general x1, matrix products, one_block(): jnp.einsum('hck,khd->chd', weights, value_block, preferred_element_type=j...  3.2 us
    ppermute x1, starting transfers between devices, collect(): theirs = lax.ppermute(grown, axis, [(d, d ^ reach) for d in range(ways)])  2.97 us
  transfers between devices with their start and end apart: 3, of which 3 were waited for; matrix products, arithmetic and copies ran while one was open for 8% of the time, Pallas kernels for 0%

profile of v1, /device:TPU:0, one launch (start us, length us, event | category | flops | bytes accessed | tf_op | source)
XLA Modules:
  0.0 110.9 jit_solution(482676795490265480)
XLA Ops:
  6.5 3.0 %collective-permute-start = (bf16[1024,2,512]{2,1,0:T(2,128)(2,1)}, bf16[1024,2,512]{2,1,0:T(2,128)(2,1)}, u32[]{:S(2)}, u32[]{:S(2)}) collective-permute-start(bf16[1024,2,512]{2,1,0:T(2,128)(2,1)} %param.8), channel_id=1, source_target_pairs={{0,4},{4,0},{1,5},{5,1},{2,6},{6,2},{3,7},{7,3},{8,12},{12,8},{9,1... | collective-permute-start | bytes 6291464 | tf_op jit(solution)/shard_map/ppermute | solution.py:14
  9.5 0.7 compare_select_fusion
  10.2 2.7 %gather_fusion = bf16[4,64,2,1024]{3,2,1,0:T(2,128)(2,1)S(1)} fusion(bf16[4,64,2,1024]{3,2,1,0:T(2,128)(2,1)S(1)} %copy-done, s32[1024]{0:T(1024)S(1)} %pad_clamp_fusion), kind=kCustom, calls=%fused_computation | custom fusion | bytes 2097168 | tf_op jit(solution)/shard_map/jit(_take)/gather | solution.py:67
  12.8 0.7 compare_and_fusion
  13.5 2.0 %broadcast_select_fusion.1 = bf16[4,64,2,1024]{3,2,1,0:T(2,128)(2,1)} fusion(bf16[4,64,2,1024]{3,2,1,0:T(2,128)(2,1)S(1)} %gather_fusion, pred[4]{0:T(512)(128)(4,1)S(1)} %compare_and_fusion), kind=kLoop, calls=%fused_computation.4 | loop fusion | flops 524288 | bytes 2097156 | tf_op jit(solution)/shard_map/jit(_take)/select_n | solution.py:67
  15.5 3.5 %all-to-all-start = ((bf16[4,64,2,1024]{3,2,1,0:T(2,128)(2,1)}), bf16[4,64,2,1024]{3,2,1,0:T(2,128)(2,1)S(1)}, u32[]{:S(2)}, u32[]{:S(2)}) async-start(bf16[4,64,2,1024]{3,2,1,0:T(2,128)(2,1)} %broadcast_select_fusion.1), calls=%async_computation | async-start | bytes 2097152 | tf_op jit(solution)/shard_map/all_to_all | solution.py:69
  19.1 0.6 dynamic_slice.11
  21.6 0.6 dynamic_slice.12
  22.9 0.7 compare_convert_fusion
  23.5 9.9 %all-to-all-done = bf16[4,64,2,1024]{3,2,1,0:T(2,128)(2,1)S(1)} async-done(((bf16[4,64,2,1024]{3,2,1,0:T(2,128)(2,1)}), bf16[4,64,2,1024]{3,2,1,0:T(2,128)(2,1)S(1)}, u32[]{:S(2)}, u32[]{:S(2)}) %all-to-all-start) | async-done | bytes 1048608 | tf_op jit(solution)/shard_map/all_to_all | solution.py:69
  33.4 0.3 copy.19
  33.8 0.2 copy.20
  34.0 1.0 copy.21
  35.0 20.5 %collective-permute-done = bf16[1024,2,512]{2,1,0:T(2,128)(2,1)} collective-permute-done((bf16[1024,2,512]{2,1,0:T(2,128)(2,1)}, bf16[1024,2,512]{2,1,0:T(2,128)(2,1)}, u32[]{:S(2)}, u32[]{:S(2)}) %collective-permute-start) | collective-permute-done | bytes 2097184 | tf_op jit(solution)/shard_map/ppermute | solution.py:14
  55.5 8.2 %broadcast_select_fusion = bf16[1024,2,1024]{2,1,0:T(2,128)(2,1)S(1)} fusion(pred[]{:T(512)S(6)} %eq.3, bf16[1024,2,512]{2,1,0:T(2,128)(2,1)} %collective-permute-done, bf16[1024,2,512]{2,1,0:T(2,128)(2,1)} %param.8), kind=kLoop, calls=%fused_computation.1 | loop fusion | flops 18874368 | bytes 8388609 | tf_op jit(solution)/shard_map/jit(_where)/select_n | solution.py:17
  63.7 1.4 %copy.27 = bf16[128,8,2,1024]{3,1,2,0:T(8,128)(2,1)S(1)} copy(bf16[128,8,2,1024]{3,2,1,0:T(2,128)(2,1)S(1)} %bitcast.23) | data formatting | bytes 8388608
  65.1 1.3 %convolution_bitcast_fusion = f32[128,2048]{0,1:T(8,128)S(1)} fusion(bf16[1024,2048]{1,0:T(8,128)(2,1)S(1)} %bitcast.22, bf16[1,128,1024]{2,1,0:T(8,128)(2,1)S(1)} %copy-done.1), kind=kOutput, calls=%fused_computation.2 | convolution fusion | flops 536870912 | bytes 5505024 | tf_op jit(solution)/shard_map/dot_general | solution.py:75
  66.5 8.2 %all_gather.3 = bf16[256,1024]{0,1:T(8,128)(2,1)S(1)} all-gather(bf16[128,1024]{0,1:T(8,128)(2,1)S(1)} %slice.29), channel_id=1, replica_groups=mesh['store'=4,'blk'=2,'batch'=4] {'blk'}, dimensions={0}, use_global_device_ids=true | all-gather | bytes 786432 | tf_op jit(solution)/shard_map/all_gather | solution.py:80
  74.7 3.2 %fusion = f32[8,128,256]{2,1,0:T(8,128)} fusion(bf16[256,8,128]{0,2,1:T(8,128)(2,1)S(1)} %bitcast.27, bf16[256,8,128]{0,2,1:T(8,128)(2,1)S(1)} %bitcast.26, bf16[256,8,128]{0,2,1:T(8,128)(2,1)} %bitcast.28, f32[]{:T(128)S(6)} %convert_element_type.32, f32[256]{0:T(256)S(1)} %compare_convert_fusion), kind=kOutput, calls=%fused_computation.5 | convolution fusion | flops 272629760 | bytes 2622468 | tf_op jit(solution)/shard_map/while/body/eval_jaxpr/hck,khd->chd/dot_general | solution.py:46
  77.9 21.6 %reduce-scatter.2.cloned.1.call-done = f32[128,1024]{0,1:T(8,128)} async-done(((f32[256,1024]{0,1:T(8,128)}), f32[128,1024]{0,1:T(8,128)}) %reduce-scatter.2.cloned.1.call-update) | async-done | bytes 524304 | tf_op jit(solution)/shard_map/reduce_scatter | solution.py:81
  99.5 1.2 %convert_reduce_fusion = f32[128]{0:T(128)S(1)} fusion(f32[128,1024]{0,1:T(8,128)} %reduce-scatter.2.cloned.1.call-done), kind=kLoop, calls=%fused_computation.11 | loop fusion | flops 393088 | bytes 524800 | tf_op jit(solution)/shard_map/reduce_sum | solution.py:57
  100.7 1.2 %fusion.7 = f32[128]{0:T(128)S(1)} fusion(f32[128]{0:T(128)S(1)} %broadcast_multiply_fusion, f32[128,1024]{0,1:T(8,128)} %reduce-scatter.2.cloned.1.call-done), kind=kLoop, calls=%fused_computation.14 | loop fusion | flops 655232 | bytes 525312 | tf_op jit(solution)/shard_map/reduce_sum | solution.py:58
  101.9 1.3 %fusion.12 = bf16[1,128,1024]{1,2,0:T(8,128)(2,1)S(1)} fusion(f32[128,2048]{0,1:T(8,128)S(1)} %convolution_bitcast_fusion, f32[1024]{0:T(1024)S(1)} %copy-done.2, f32[128]{0:T(128)S(1)} %add_rsqrt_fusion, f32[128]{0:T(128)S(1)} %broadcast_multiply_fusion, f32[128,1024]{0,1:T(8,128)} %reduce-scatter.2.cloned.1.call-done), kind=kLoop, calls=%fused_computation.21 | loop fusion | flops 1703936 | bytes 1315840 | tf_op jit(solution)/shard_map/broadcast_in_dim | solution.py:84
  103.2 0.9 copy.24
  (17 shorter events, 0.2 us)
Async XLA Ops:
  6.5 3.6 %copy-start = (bf16[4,64,2,1024]{3,2,1,0:T(2,128)(2,1)S(1)}, bf16[4,64,2,1024]{3,2,1,0:T(2,128)(2,1)}, u32[]{:S(2)}) copy-start(bf16[4,64,2,1024]{3,2,1,0:T(2,128)(2,1)} %param.7) | copy-start | bytes 3145732
  6.5 12.5 %copy-start.3 = (s32[4]{0:T(128)S(1)}, s32[4]{0:T(128)}, u32[]{:S(2)}) copy-start(s32[4]{0:T(128)} %param.10) | copy-start | bytes 52
  6.5 15.1 %copy-start.4 = (s32[4]{0:T(128)S(1)}, s32[4]{0:T(128)}, u32[]{:S(2)}) copy-start(s32[4]{0:T(128)} %param.11) | copy-start | bytes 52
  6.5 48.9 %collective-permute-start = (bf16[1024,2,512]{2,1,0:T(2,128)(2,1)}, bf16[1024,2,512]{2,1,0:T(2,128)(2,1)}, u32[]{:S(2)}, u32[]{:S(2)}) collective-permute-start(bf16[1024,2,512]{2,1,0:T(2,128)(2,1)} %param.8), channel_id=1, source_target_pairs={{0,4},{4,0},{1,5},{5,1},{2,6},{6,2},{3,7},{7,3},{8,12},{12,8},{9,1... | collective-permute-start | bytes 6291464 | tf_op jit(solution)/shard_map/ppermute | solution.py:14
  15.5 18.0 %all-to-all-start = ((bf16[4,64,2,1024]{3,2,1,0:T(2,128)(2,1)}), bf16[4,64,2,1024]{3,2,1,0:T(2,128)(2,1)S(1)}, u32[]{:S(2)}, u32[]{:S(2)}) async-start(bf16[4,64,2,1024]{3,2,1,0:T(2,128)(2,1)} %broadcast_select_fusion.1), calls=%async_computation | async-start | bytes 2097152 | tf_op jit(solution)/shard_map/all_to_all | solution.py:69
  19.0 80.5 %reduce-scatter.2.cloned.1.call-start = ((), (), s32[]{:S(2)}) async-start(), calls=%async_computation.2 | async-start | bytes 1572864 | tf_op jit(solution)/shard_map/reduce_scatter | solution.py:81
  63.6 1.5 %copy-start.1 = (bf16[1,128,1024]{2,1,0:T(8,128)(2,1)S(1)}, bf16[1,128,1024]{2,1,0:T(8,128)(2,1)}, u32[]{:S(2)}) copy-start(bf16[1,128,1024]{2,1,0:T(8,128)(2,1)} %param.6) | copy-start | bytes 786436
  74.7 27.2 %copy-start.2 = (f32[1024]{0:T(1024)S(1)}, f32[1024]{0:T(1024)}, u32[]{:S(2)}) copy-start(f32[1024]{0:T(1024)} %param.9) | copy-start | bytes 12292
Sparse Core Ops, SparseCore 0:
  78.0 21.4 reduce-scatter.1
